TPU v7x, 32 devices: a whole 2x2x4 slice. The times are simulated.
32 devices in a mesh: seq: 8 (over z, y), exp: 4 (over x, core).
Axes of the slice: x: 2, y: 2, z: 4, core: 2. Of those that a mesh axis runs over, the one named last changes fastest.
Arguments:
- hidden: bfloat16 [4, 1024, 2048], P('exp', 'seq'), may hold values from -6 to 6
- lengths: int32 [4, 4], P('exp'), may hold values from 1 to 512, 1024 in all within a row
- attn_gain: float32 [2048], replicated, may hold values from 0 to 10
- w_qkv: bfloat16 [2048, 3, 16, 128], P(None, None, 'seq'), may hold values from -0.125 to 0.125
- w_out: bfloat16 [16, 128, 2048], P('seq'), may hold values from -0.125 to 0.125
- moe_gain: float32 [2048], replicated, may hold values from 0.5 to 1.5
- router: bfloat16 [2048, 16], replicated, may hold values from -8 to 8
- routes: int32 [4, 1024, 6], P('exp', 'seq'), may hold values from 0 to 15, all different within a row; in each aligned block of 128 rows (0 to 127, 128 to 255, ..., all dimensions but the last counted through in order) at most 56 rows name the same one
- w_gate_up: bfloat16 [32, 2, 704, 2048], P(('seq', 'exp')), may hold values from -0.125 to 0.125
- w_down: bfloat16 [32, 704, 2048], P(('seq', 'exp')), may hold values from -0.15625 to 0.15625
- final_gain: float32 [2048], replicated, may hold values from 0.5 to 1.5
- lm_head: bfloat16 [102400, 2048], P(('seq', 'exp')), may hold values from -4 to 4
Outputs:
- layer_out: bfloat16 [4, 1024, 2048], P('exp', 'seq')
- logprobs: float32 [16, 102400], P(None, ('seq', 'exp'))
Inputs may be any that keep to these rules, and one draw needn't show every extreme that they name: `routes`: in the rows of one device no expert is named by more than 56 rows; in some devices one expert is named by exactly 56 rows. `lengths`: each row sums to 1024; its largest entry is 512.
All inputs are finite; a program needn't handle non-finite values.
Results may differ from a plain program's by a relative error of at most 0.0095.
The roundings to bfloat16 on the way count: a program that leaves them out, or rounds other values in their place, can miss the bound.
Values may be sent and summed in bfloat16 or wider, within the bound.
No kernel may reach another device: no remote copies, remote signals or barrier semaphores. Data moves between devices by JAX's collectives and lax.ppermute only.
A program may use at most 128 MiB of HBM per device.

v0:
```python
import jax
import jax.numpy as jnp
from jax import lax
from jax.sharding import PartitionSpec as P

epsilon = 1e-06


def joined(value, axis, join):
    pieces = jax.tree.map(lambda part: lax.all_gather(part, axis), value)
    head = jax.tree.map(lambda part: part[0], pieces)
    tail = jax.tree.map(lambda part: part[1:], pieces)
    subtotal, _ = lax.scan(lambda subtotal, piece: (join(subtotal, piece), None), head, tail)
    return subtotal


def rms_scale(values, gain):
    widened = values.astype(jnp.float32)
    inverse = lax.rsqrt(jnp.mean(widened * widened, axis=-1, keepdims=True) + epsilon)
    return widened * inverse * gain


def segment_layout(prompt_lengths, count):
    ends = jnp.cumsum(prompt_lengths)
    starts = ends - prompt_lengths
    places = jnp.arange(count, dtype=jnp.int32)
    member = ((places[:, None] >= starts[None, :]) & (places[:, None] < ends[None, :])).astype(
        jnp.int32
    )
    numbers = jnp.arange(prompt_lengths.shape[0], dtype=jnp.int32)
    segment = jnp.sum(member * numbers[None, :], axis=1)
    offset = places - jnp.sum(member * starts[None, :], axis=1)
    return (segment, offset)


def rotary(values, positions):
    half_size = values.shape[-1] // 2
    freqs = 10000.0 ** (-2.0 * jnp.arange(half_size, dtype=jnp.float32) / values.shape[-1])
    angles = positions.astype(jnp.float32)[:, None] * freqs[None, :]
    cosine = jnp.cos(angles)[:, None, :]
    sine = jnp.sin(angles)[:, None, :]
    first_half = values[..., :half_size]
    second_half = values[..., half_size:]
    return jnp.concatenate(
        [first_half * cosine - second_half * sine, second_half * cosine + first_half * sine],
        axis=-1,
    )


def merge_softmax(earlier, later):
    highest = jnp.maximum(earlier[0], later[0])
    return (
        highest,
        earlier[1] * jnp.exp(earlier[0] - highest) + later[1] * jnp.exp(later[0] - highest),
    )


def per_device(
    hidden,
    lengths,
    attn_gain,
    w_qkv,
    w_out,
    moe_gain,
    router,
    routes,
    w_gate_up,
    w_down,
    final_gain,
    lm_head,
):
    seq_count = lax.axis_size("seq")
    group_count = lax.axis_size("exp")
    device_count = seq_count * group_count
    token_rows = hidden[0]
    tok_rows = token_rows.shape[0]
    model_width = token_rows.shape[1]
    group_tokens = tok_rows * seq_count
    head_count = w_qkv.shape[2]
    head_size = w_qkv.shape[3]
    scale_factor = head_size ** (-0.5)
    prompt_lengths = lengths[0]
    segment, offset = segment_layout(prompt_lengths, group_tokens)
    normed = rms_scale(token_rows, attn_gain).astype(jnp.bfloat16)
    qkv_weight = w_qkv.reshape(model_width, 3 * head_count * head_size)
    qkv = jnp.dot(
        lax.all_gather(normed, "seq", axis=0, tiled=True),
        qkv_weight,
        preferred_element_type=jnp.float32,
    ).reshape(group_tokens, 3, head_count, head_size)
    query = rotary(qkv[:, 0], offset).astype(jnp.bfloat16)
    keys = rotary(qkv[:, 1], offset).astype(jnp.bfloat16)
    values = qkv[:, 2].astype(jnp.bfloat16)
    block_rows = min(512, group_tokens)
    key_places = jnp.arange(group_tokens, dtype=jnp.int32)

    def one_block(block_index):
        first_row = block_index * block_rows
        block_query = lax.dynamic_slice_in_dim(query, first_row, block_rows, 0)
        block_segment = lax.dynamic_slice_in_dim(segment, first_row, block_rows, 0)
        query_places = first_row + jnp.arange(block_rows, dtype=jnp.int32)
        scores = (
            jnp.einsum("qhd,khd->hqk", block_query, keys, preferred_element_type=jnp.float32)
            * scale_factor
        )
        allowed = (block_segment[:, None] == segment[None, :]) & (
            key_places[None, :] <= query_places[:, None]
        )
        scores = jnp.where(allowed[None], scores, -1e30)
        highest = jnp.max(scores, axis=2, keepdims=True)
        weights = jnp.exp(scores - highest)
        probs = (weights / jnp.sum(weights, axis=2, keepdims=True)).astype(jnp.bfloat16)
        return jnp.einsum("hqk,khd->qhd", probs, values, preferred_element_type=jnp.float32).astype(
            jnp.bfloat16
        )

    blocks = lax.map(one_block, jnp.arange(group_tokens // block_rows, dtype=jnp.int32))
    heads_flat = blocks.reshape(group_tokens, head_count * head_size)
    regrouped = lax.all_to_all(heads_flat, "seq", split_axis=0, concat_axis=1, tiled=True)
    full_weight = lax.all_gather(w_out, "seq", axis=0, tiled=True).reshape(-1, model_width)
    mixed = jnp.dot(regrouped, full_weight, preferred_element_type=jnp.float32)
    middle = (token_rows.astype(jnp.float32) + mixed).astype(jnp.bfloat16)
    expert_in = rms_scale(middle, moe_gain).astype(jnp.bfloat16)
    logits = jnp.dot(expert_in, router, preferred_element_type=jnp.float32)
    expert_count = router.shape[1]
    token_routes = routes[0]
    top_count = token_routes.shape[1]
    expert_ids = jnp.arange(expert_count, dtype=jnp.int32)
    chosen_mask = token_routes[:, :, None] == expert_ids[None, None, :]
    chosen = jnp.sum(jnp.where(chosen_mask, logits[:, None, :], 0.0), axis=2)
    gates = jax.nn.softmax(chosen, axis=-1)
    capacity = max(2, tok_rows * top_count * 7 // (6 * expert_count))
    flat_mask = chosen_mask.reshape(tok_rows * top_count, expert_count).astype(jnp.int32)
    earlier_count = jnp.cumsum(flat_mask, axis=0) - flat_mask
    slot_index = jnp.sum(earlier_count * flat_mask, axis=1)
    target = (token_routes.reshape(-1) * capacity + slot_index).reshape(tok_rows, top_count)
    slot_total = expert_count * capacity
    placed = target[:, :, None] == jnp.arange(slot_total, dtype=jnp.int32)[None, None, :]
    dispatch_table = jnp.any(placed, axis=1).astype(jnp.bfloat16)
    slot_weights = jnp.sum(jnp.where(placed, gates[:, :, None], 0.0), axis=1)
    packed = lax.dot_general(
        dispatch_table, expert_in, (((0,), (0,)), ((), ())), preferred_element_type=jnp.float32
    ).astype(jnp.bfloat16)
    shares = device_count // expert_count
    outgoing = jnp.broadcast_to(
        packed.reshape(expert_count, 1, capacity, model_width),
        (expert_count, shares, capacity, model_width),
    )
    outgoing = outgoing.reshape(device_count, capacity, model_width)
    gate_up = w_gate_up[0]
    down_weight = w_down[0]
    arrived = lax.all_to_all(outgoing, ("seq", "exp"), split_axis=0, concat_axis=0, tiled=True)
    arrived_shape = arrived.shape
    flat_rows = arrived.reshape(-1, model_width)
    both = jnp.einsum("rd,gfd->rgf", flat_rows, gate_up, preferred_element_type=jnp.float32)
    act = (jax.nn.silu(both[:, 0]) * both[:, 1]).astype(jnp.bfloat16)
    part = jnp.dot(act, down_weight, preferred_element_type=jnp.float32).astype(jnp.bfloat16)
    returned = lax.all_to_all(
        part.reshape(arrived_shape), ("seq", "exp"), split_axis=0, concat_axis=0, tiled=True
    )
    summed = jnp.sum(
        returned.reshape(expert_count, shares, capacity, model_width).astype(jnp.float32), axis=1
    )
    summed = summed.reshape(slot_total, model_width)
    routed = jnp.dot(
        slot_weights, summed, precision=lax.Precision.HIGHEST, preferred_element_type=jnp.float32
    )
    layer_rows = (middle.astype(jnp.float32) + routed).astype(jnp.bfloat16)
    prompt_count = prompt_lengths.shape[0]
    last_places = jnp.cumsum(prompt_lengths) - 1
    here_places = lax.axis_index("seq") * tok_rows + jnp.arange(tok_rows, dtype=jnp.int32)
    select_table = (last_places[:, None] == here_places[None, :]).astype(jnp.bfloat16)
    picked = jnp.dot(select_table, layer_rows, preferred_element_type=jnp.float32)
    board = jnp.zeros((group_count * prompt_count, model_width), jnp.float32)
    board = lax.dynamic_update_slice_in_dim(board, picked, lax.axis_index("exp") * prompt_count, 0)
    last_rows = lax.psum(board, ("seq", "exp"))
    final = rms_scale(last_rows, final_gain).astype(jnp.bfloat16)
    vocab_scores = lax.dot_general(
        final, lm_head, (((1,), (1,)), ((), ())), preferred_element_type=jnp.float32
    )
    local_peak = jnp.max(vocab_scores, axis=1)
    local_total = jnp.sum(jnp.exp(vocab_scores - local_peak[:, None]), axis=1)
    global_peak, global_total = joined((local_peak, local_total), ("seq", "exp"), merge_softmax)
    logprobs = vocab_scores - (global_peak + jnp.log(global_total))[:, None]
    return (layer_rows[None], logprobs)


def solution(mesh):
    return jax.shard_map(
        per_device,
        mesh=mesh,
        in_specs=(
            P("exp", "seq", None),
            P("exp", None),
            P(),
            P(None, None, "seq", None),
            P("seq", None, None),
            P(),
            P(),
            P("exp", "seq", None),
            P(("seq", "exp"), None, None, None),
            P(("seq", "exp"), None, None),
            P(),
            P(("seq", "exp"), None),
        ),
        out_specs=(P("exp", "seq", None), P(None, ("seq", "exp"))),
        check_vma=False,
    )
```

profile of v0, /device:TPU:0, one launch (start us, length us, event | category | flops | bytes accessed | tf_op | source)
XLA Modules:
  0.0 774.0 jit_solution(13950051054370654755)
XLA Ops:
  7.2 1.4 fusion.43
  8.6 2.0 fusion.45
  10.7 0.7 all-gather.7.cloned.1.call-update
  11.4 0.8 reduce-window.10
  12.3 8.1 %reshape.273 = bf16[2048,768]{1,0:T(8,128)(2,1)} reshape(bf16[2048,3,2,128]{3,2,1,0:T(2,128)(2,1)} %param.19) | data formatting | bytes 6291456 | tf_op jit(solution)/shard_map/reshape | solution.py:85
  20.3 4.8 copy.43
  25.3 1.0 multiply_cosine_fusion
  26.3 60.7 %all-gather.5.cloned.1.call-done = bf16[1024,2048]{1,0:T(8,128)(2,1)} async-done(((bf16[128,2048]{1,0:T(8,128)(2,1)}), bf16[1024,2048]{1,0:T(8,128)(2,1)}) %all-gather.5.cloned.1.call-update) | async-done | bytes 4194320 | tf_op jit(solution)/shard_map/all_gather | solution.py:87
  86.9 6.2 fusion.34
  93.1 0.1 slice_bitcast_fusion
  93.3 0.4 subtract_convert_fusion
  93.6 1.3 pad_maximum_fusion
  95.0 1.1 copy.45
  96.0 1.3 fusion.46
  97.4 1.0 copy.46
  98.4 21.8 %while.24 = (s32[]{:T(128)}, bf16[2,512,2,128]{3,2,1,0:T(2,128)(2,1)}, s32[2]{0:T(128)S(1)}, s32[1024]{0:T(1024)S(1)}, bf16[1024,2,128]{0,2,1:T(8,128)(2,1)}, /*...) while((s32[]{:T(128)}, ...), condition=%wide.region_7.8_spmd.clone, body=%wide.region_4.7_spmd.clone.sunk | while | flops 544867840 | bytes 15751407 | solution.py:117
  98.4 0.6 dynamic_slice.53
  99.6 0.6 fusion.95
  100.2 4.9 fusion.96
  105.0 3.1 fusion.97
  108.2 0.3 copy_dynamic-update-slice_fusion.2
  108.5 0.8 copy-done.9
  109.3 0.6 dynamic_slice.53
  110.5 0.6 fusion.95
  111.1 4.9 fusion.96
  115.9 3.1 fusion.97
  119.1 0.3 copy_dynamic-update-slice_fusion.2
  119.4 0.8 copy-done.9
  120.2 2.3 all_to_all.20
  122.5 4.3 all-to-all-start
  127.2 0.6 fusion.54
  127.8 3.2 reduce-window.11
  131.0 0.2 slice_reduce_fusion
  131.6 0.6 fusion.48
  132.2 0.9 copy.53
  133.1 0.5 fusion.37
  133.6 11.9 %all-to-all-done = bf16[8,128,256]{2,1,0:T(8,128)(2,1)} async-done(((bf16[8,128,256]{2,1,0:T(8,128)(2,1)}), bf16[8,128,256]{2,1,0:T(8,128)(2,1)}, u32[]{:S(2)}, u32[]{:S(2)}) %all-to-all-start) | async-done | bytes 524320 | tf_op jit(solution)/shard_map/all_to_all | solution.py:119
  145.4 2.0 copy.48
  147.5 73.1 %all-gather.7.cloned.1.call-done = bf16[16,128,2048]{2,1,0:T(8,128)(2,1)} async-done(((bf16[2,128,2048]{2,1,0:T(8,128)(2,1)}), bf16[16,128,2048]{2,1,0:T(8,128)(2,1)}) %all-gather.7.cloned.1.call-update) | async-done | bytes 8388624 | tf_op jit(solution)/shard_map/all_gather | solution.py:120
  220.6 4.9 multiply_reduce_fusion
  225.5 3.0 convolution_convert_fusion.1
  228.5 3.2 broadcast_in_dim.59
  231.7 163.6 %all_to_all.29 = bf16[32,56,2048]{2,1,0:T(8,128)(2,1)S(1)} all-to-all(bf16[32,56,2048]{2,1,0:T(8,128)(2,1)S(1)} %bitcast.119), channel_id=1, replica_groups=mesh['seq'=8,'exp'=4] {'seq','exp'}, dimensions={0} | all-to-all | bytes 14680064 | tf_op jit(solution)/shard_map/all_to_all | solution.py:152
  395.3 12.7 %fusion.31 = f32[1792,2,704]{0,2,1:T(8,128)S(1)} fusion(bf16[1792,2048,1]{1,0,2:T(8,128)(2,1)S(1)} %bitcast.124, bf16[1,2,704,2048]{3,2,1,0:T(8,128)(2,1)} %param.24), kind=kOutput, calls=%fused_computation.33 | convolution fusion | flops 10334765056 | bytes 23199744 | tf_op jit(solution)/shard_map/rd,gfd->rgf/dot_general | solution.py:155
  408.1 8.2 %convolution_convert_fusion = bf16[1792,2048]{1,0:T(8,128)(2,1)} fusion(bf16[1,704,2048]{2,1,0:T(8,128)(2,1)S(1)} %copy-done, f32[1792,2,704]{0,2,1:T(8,128)S(1)} %fusion.31), kind=kOutput, calls=%fused_computation.32 | convolution fusion | flops 5178621952 | bytes 20316160 | tf_op jit(solution)/shard_map/dot_general | solution.py:157
  416.3 3.9 all-to-all-start.2
  420.3 0.3 all-reduce.5.cloned.1.call-start
  420.6 1.5 fusion.63
  422.2 1.1 select_reduce_fusion
  423.3 160.0 %all-to-all-done.2 = bf16[32,56,2048]{2,1,0:T(8,128)(2,1)} async-done(((bf16[32,56,2048]{2,1,0:T(8,128)(2,1)}), bf16[32,56,2048]{2,1,0:T(8,128)(2,1)}, u32[]{:S(2)}, u32[]{:S(2)}) %all-to-all-start.2) | async-done | bytes 7340064 | tf_op jit(solution)/shard_map/all_to_all | solution.py:158
  583.4 5.5 convert_reduce_fusion
  588.9 4.2 fusion.42
  593.2 0.2 convolution_dynamic-update-slice_fusion
  593.4 0.7 copy-done.10
  594.1 120.0 %all-reduce.5.cloned.1.call-done = f32[16,2048]{1,0:T(8,128)} async-done(((f32[16,2048]{1,0:T(8,128)}), f32[16,2048]{1,0:T(8,128)}) %all-reduce.5.cloned.1.call-update) | async-done | bytes 131088 | tf_op jit(solution)/shard_map/psum | solution.py:176
  714.1 1.0 multiply_reduce_fusion.1
  715.2 8.4 %fusion.70 = (f32[16]{0:T(128)S(1)}, f32[16,3200]{1,0:T(8,128)S(1)}) fusion(bf16[3200,2048]{1,0:T(8,128)(2,1)} %param.27, f32[16,2048]{1,0:T(8,128)} %all-reduce.5.cloned.1.call-done, f32[2048]{0:T(1024)S(1)} %copy-done.14, f32[16]{0:T(128)S(1)} %add_rsqrt_fusion), kind=kOutput, calls=%fused_computation.115 | convolution fusion | flops 209864688 | bytes 13451392 | tf_op jit(solution)/shard_map/dot_general | solution.py:178
  723.6 0.7 copy-done.6
  724.3 0.2 exponential_reduce_fusion
  724.5 0.2 dynamic-update-slice
  724.8 0.2 dynamic-update-slice.1
  725.0 39.2 %all-reduce.2 = (f32[512]{0:T(512)S(1)}, f32[512]{0:T(512)S(1)}) all-reduce(f32[512]{0:T(512)S(1)} %dynamic-update-slice, f32[512]{0:T(512)S(1)} %dynamic-update-slice.1), channel_id=2, replica_groups=mesh['seq'=8,'exp'=4] {'seq','exp'}, use_global_device_ids=true, to_apply=%add | all-reduce | flops 1024 | bytes 8192
  764.4 1.3 while.23
  765.8 1.7 broadcast_subtract_fusion
  (107 shorter events, 2.4 us)
Async XLA Ops:
  7.2 400.9 %copy-start = (bf16[1,704,2048]{2,1,0:T(8,128)(2,1)S(1)}, bf16[1,704,2048]{2,1,0:T(8,128)(2,1)}, u32[]{:S(2)}) copy-start(bf16[1,704,2048]{2,1,0:T(8,128)(2,1)} %param.25) | copy-start | bytes 8650756
  7.2 79.7 %all-gather.5.cloned.1.call-start = ((), (), s32[]{:S(2)}) async-start(), calls=%async_computation.3 | async-start | bytes 4718592 | tf_op jit(solution)/shard_map/all_gather | solution.py:87
  10.7 209.9 %all-gather.7.cloned.1.call-start = ((), (), s32[]{:S(2)}) async-start(), calls=%async_computation.4 | async-start | bytes 9437184 | tf_op jit(solution)/shard_map/all_gather | solution.py:120
  12.3 12.9 %copy-start.15 = (s32[4,1]{0,1:T(1,128)}, s32[4,1]{0,1:T(1,128)S(1)}, u32[]{:S(2)}) copy-start(s32[4,1]{0,1:T(1,128)S(1)} %reduce-window.10) | copy-start | bytes 52
  20.3 4.8 copy-start.17
  93.1 1.9 copy-start.4
  98.4 28.4 %copy-start.13 = (s32[1,128,6]{1,0,2:T(1,128)S(1)}, s32[1,128,6]{1,0,2:T(1,128)}, u32[]{:S(2)}) copy-start(s32[1,128,6]{1,0,2:T(1,128)} %param.23) | copy-start | bytes 9220
  105.0 3.1 copy-start.8
  108.5 0.8 copy-start.9
  115.9 3.1 copy-start.8
  119.4 0.8 copy-start.9
  120.2 100.4 %copy-start.3 = (bf16[1,128,2048]{2,1,0:T(8,128)(2,1)S(1)}, bf16[1,128,2048]{2,1,0:T(8,128)(2,1)}, u32[]{:S(2)}) copy-start(bf16[1,128,2048]{2,1,0:T(8,128)(2,1)} %param.16) | copy-start | bytes 1572868
  122.5 23.0 %all-to-all-start = ((bf16[8,128,256]{2,1,0:T(8,128)(2,1)}), bf16[8,128,256]{2,1,0:T(8,128)(2,1)}, u32[]{:S(2)}, u32[]{:S(2)}) async-start(bf16[8,128,256]{2,1,0:T(8,128)(2,1)} %all_to_all.20), calls=%async_computation | async-start | bytes 1048576 | tf_op jit(solution)/shard_map/all_to_all | solution.py:119
  220.6 5.0 copy-start.12
  225.5 3.0 copy-start.1
  416.3 4.3 copy-start.16
  416.3 4.3 copy-start.11
  416.3 167.0 %all-to-all-start.2 = ((bf16[32,56,2048]{2,1,0:T(8,128)(2,1)}), bf16[32,56,2048]{2,1,0:T(8,128)(2,1)}, u32[]{:S(2)}, u32[]{:S(2)}) async-start(bf16[32,56,2048]{2,1,0:T(8,128)(2,1)} %bitcast.123), calls=%async_computation.2 | async-start | bytes 14680064 | tf_op jit(solution)/shard_map/all_to_all | solution.py:158
  420.3 293.9 %all-reduce.5.cloned.1.call-start = ((), (), s32[]{:S(2)}) async-start(), calls=%async_computation.5 | async-start | bytes 262144 | tf_op jit(solution)/shard_map/psum | solution.py:176
  583.4 5.5 copy-start.2
  583.4 5.5 copy-start.7
  588.9 126.3 %copy-start.14 = (f32[2048]{0:T(1024)S(1)}, f32[2048]{0:T(1024)}, u32[]{:S(2)}) copy-start(f32[2048]{0:T(1024)} %param.26) | copy-start | bytes 24580
  593.1 130.5 %copy-start.5 = (bf16[128,2048]{1,0:T(8,128)(2,1)}, bf16[128,2048]{1,0:T(8,128)(2,1)S(1)}, u32[]{:S(2)}) copy-start(bf16[128,2048]{1,0:T(8,128)(2,1)S(1)} %fusion.42) | copy-start | bytes 1572868
  593.4 0.7 copy-start.10
  723.6 0.7 copy-start.6
Sparse Core Ops, SparseCore 0:
  10.8 76.0 all-gather.4
  89.0 131.4 all-gather.6
  594.2 119.8 all-reduce.4
where the time goes:
time: 775 us; the launch traced here: 774 us
  waiting for transfers between devices  426 us (55%)
  blocking collectives  203 us (26%)
  matrix products  65.4 us (8%)
  local copies, waits for them, and re-layouts  31.1 us (4%)
  other arithmetic  23.9 us (3%)
  between operations  14.1 us (2%)
  starting transfers between devices  8.62 us (1%)
    all_to_all x1, blocking collectives, per_device(): lax.all_to_all(outgoing, ('seq', 'exp'), split_axis=0, concat_axis=0, til...  164 us
    all_to_all x1, waiting for transfers between devices, per_device(): lax.all_to_all(part.reshape(arrived_shape), ('seq', 'exp'), split_axis=0,...  160 us
    psum x1, waiting for transfers between devices, per_device(): last_rows = lax.psum(board, ('seq', 'exp'))  120 us
    all_gather x1, waiting for transfers between devices, per_device(): lax.all_gather(w_out, 'seq', axis=0, tiled=True).reshape(-1, model_width)  73.1 us
    all_gather x1, waiting for transfers between devices, per_device(): lax.all_gather(normed, 'seq', axis=0, tiled=True)  60.7 us
    unnamed x1, blocking collectives  39.2 us
  transfers between devices with their start and end apart: 5, of which 5 were waited for; matrix products, arithmetic and copies ran while one was open for 7% of the time, Pallas kernels for 0%

commit v1 on v0

--- a/solution.py
+++ b/solution.py
@@ -173,7 +173,7 @@
     picked = jnp.dot(select_table, layer_rows, preferred_element_type=jnp.float32)
     board = jnp.zeros((group_count * prompt_count, model_width), jnp.float32)
     board = lax.dynamic_update_slice_in_dim(board, picked, lax.axis_index("exp") * prompt_count, 0)
-    last_rows = lax.psum(board, ("seq", "exp"))
+    last_rows = lax.psum(lax.psum(board, "exp"), "seq")
     final = rms_scale(last_rows, final_gain).astype(jnp.bfloat16)
     vocab_scores = lax.dot_general(
         final, lm_head, (((1,), (1,)), ((), ())), preferred_element_type=jnp.float32

time: 775 us -> 758 us (0.978)
  waiting for transfers between devices: 426 us -> 408 us
    psum x1 -> x2, waiting for transfers between devices: 120 us -> 102 us  [per_device(): last_rows = lax.psum(lax.psum(board, 'exp'), 'seq')]
  transfers between devices with their start and end apart: 5 -> 6, of which waited for: 5 -> 6; matrix products, arithmetic and copies ran while one was open for 7% -> 7% of each run, Pallas kernels for 0% -> 0%
where the time goes in v1:
time: 758 us; the launch traced here: 757 us
  waiting for transfers between devices  408 us (54%)
  blocking collectives  203 us (27%)
  matrix products  65.4 us (9%)
  local copies, waits for them, and re-layouts  31.1 us (4%)
  other arithmetic  23.9 us (3%)
  between operations  14.2 us (2%)
  starting transfers between devices  8.66 us (1%)
    all_to_all x1, blocking collectives, per_device(): lax.all_to_all(outgoing, ('seq', 'exp'), split_axis=0, concat_axis=0, til...  164 us
    all_to_all x1, waiting for transfers between devices, per_device(): lax.all_to_all(part.reshape(arrived_shape), ('seq', 'exp'), split_axis=0,...  160 us
    psum x2, waiting for transfers between devices, per_device(): last_rows = lax.psum(lax.psum(board, 'exp'), 'seq')  102 us
    all_gather x1, waiting for transfers between devices, per_device(): lax.all_gather(w_out, 'seq', axis=0, tiled=True).reshape(-1, model_width)  73.1 us
    all_gather x1, waiting for transfers between devices, per_device(): lax.all_gather(normed, 'seq', axis=0, tiled=True)  60.7 us
    unnamed x1, blocking collectives  39.6 us
  transfers between devices with their start and end apart: 6, of which 6 were waited for; matrix products, arithmetic and copies ran while one was open for 7% of the time, Pallas kernels for 0%

profile of v1, /device:TPU:0, one launch (start us, length us, event | category | flops | bytes accessed | tf_op | source)
XLA Modules:
  0.0 756.5 jit_solution(15383001745157966579)
XLA Ops:
  7.2 1.4 fusion.43
  8.6 2.0 fusion.45
  10.7 0.7 all-gather.7.cloned.1.call-update
  11.4 0.8 reduce-window.10
  12.3 8.1 %reshape.273 = bf16[2048,768]{1,0:T(8,128)(2,1)} reshape(bf16[2048,3,2,128]{3,2,1,0:T(2,128)(2,1)} %param.19) | data formatting | bytes 6291456 | tf_op jit(solution)/shard_map/reshape | solution.py:85
  20.3 4.8 copy.43
  25.3 1.0 multiply_cosine_fusion
  26.3 60.7 %all-gather.5.cloned.1.call-done = bf16[1024,2048]{1,0:T(8,128)(2,1)} async-done(((bf16[128,2048]{1,0:T(8,128)(2,1)}), bf16[1024,2048]{1,0:T(8,128)(2,1)}) %all-gather.5.cloned.1.call-update) | async-done | bytes 4194320 | tf_op jit(solution)/shard_map/all_gather | solution.py:87
  86.9 6.2 fusion.34
  93.3 0.4 subtract_convert_fusion
  93.6 1.3 pad_maximum_fusion
  95.0 1.1 copy.45
  96.0 1.3 fusion.46
  97.4 1.0 copy.46
  98.4 21.8 %while.24 = (s32[]{:T(128)}, bf16[2,512,2,128]{3,2,1,0:T(2,128)(2,1)}, s32[2]{0:T(128)S(1)}, s32[1024]{0:T(1024)S(1)}, bf16[1024,2,128]{0,2,1:T(8,128)(2,1)}, /*...) while((s32[]{:T(128)}, ...), condition=%wide.region_7.8_spmd.clone, body=%wide.region_4.7_spmd.clone.sunk | while | flops 544867840 | bytes 15751407 | solution.py:117
  98.4 0.6 dynamic_slice.53
  99.6 0.6 fusion.95
  100.2 4.9 fusion.96
  105.0 3.1 fusion.97
  108.2 0.3 copy_dynamic-update-slice_fusion.2
  108.5 0.8 copy-done.9
  109.3 0.6 dynamic_slice.53
  110.5 0.6 fusion.95
  111.1 4.9 fusion.96
  115.9 3.1 fusion.97
  119.1 0.3 copy_dynamic-update-slice_fusion.2
  119.4 0.8 copy-done.9
  120.2 2.3 all_to_all.20
  122.5 4.3 all-to-all-start
  127.2 0.6 fusion.54
  127.8 3.2 reduce-window.11
  131.0 0.2 slice_reduce_fusion
  131.6 0.6 fusion.48
  132.2 0.9 copy.53
  133.1 0.5 fusion.37
  133.6 11.9 %all-to-all-done = bf16[8,128,256]{2,1,0:T(8,128)(2,1)} async-done(((bf16[8,128,256]{2,1,0:T(8,128)(2,1)}), bf16[8,128,256]{2,1,0:T(8,128)(2,1)}, u32[]{:S(2)}, u32[]{:S(2)}) %all-to-all-start) | async-done | bytes 524320 | tf_op jit(solution)/shard_map/all_to_all | solution.py:119
  145.4 2.0 copy.48
  147.5 73.1 %all-gather.7.cloned.1.call-done = bf16[16,128,2048]{2,1,0:T(8,128)(2,1)} async-done(((bf16[2,128,2048]{2,1,0:T(8,128)(2,1)}), bf16[16,128,2048]{2,1,0:T(8,128)(2,1)}) %all-gather.7.cloned.1.call-update) | async-done | bytes 8388624 | tf_op jit(solution)/shard_map/all_gather | solution.py:120
  220.6 4.9 multiply_reduce_fusion
  225.5 3.0 convolution_convert_fusion.1
  228.5 3.2 broadcast_in_dim.59
  231.7 163.6 %all_to_all.29 = bf16[32,56,2048]{2,1,0:T(8,128)(2,1)S(1)} all-to-all(bf16[32,56,2048]{2,1,0:T(8,128)(2,1)S(1)} %bitcast.119), channel_id=1, replica_groups=mesh['seq'=8,'exp'=4] {'seq','exp'}, dimensions={0} | all-to-all | bytes 14680064 | tf_op jit(solution)/shard_map/all_to_all | solution.py:152
  395.3 12.7 %fusion.31 = f32[1792,2,704]{0,2,1:T(8,128)S(1)} fusion(bf16[1792,2048,1]{1,0,2:T(8,128)(2,1)S(1)} %bitcast.124, bf16[1,2,704,2048]{3,2,1,0:T(8,128)(2,1)} %param.24), kind=kOutput, calls=%fused_computation.33 | convolution fusion | flops 10334765056 | bytes 23199744 | tf_op jit(solution)/shard_map/rd,gfd->rgf/dot_general | solution.py:155
  408.1 8.2 %convolution_convert_fusion = bf16[1792,2048]{1,0:T(8,128)(2,1)} fusion(bf16[1,704,2048]{2,1,0:T(8,128)(2,1)S(1)} %copy-done, f32[1792,2,704]{0,2,1:T(8,128)S(1)} %fusion.31), kind=kOutput, calls=%fused_computation.32 | convolution fusion | flops 5178621952 | bytes 20316160 | tf_op jit(solution)/shard_map/dot_general | solution.py:157
  416.3 3.9 all-to-all-start.2
  420.3 0.3 all-reduce.6.cloned.1.call-start
  420.6 1.5 fusion.63
  422.2 1.1 select_reduce_fusion
  423.3 160.0 %all-to-all-done.2 = bf16[32,56,2048]{2,1,0:T(8,128)(2,1)} async-done(((bf16[32,56,2048]{2,1,0:T(8,128)(2,1)}), bf16[32,56,2048]{2,1,0:T(8,128)(2,1)}, u32[]{:S(2)}, u32[]{:S(2)}) %all-to-all-start.2) | async-done | bytes 7340064 | tf_op jit(solution)/shard_map/all_to_all | solution.py:158
  583.4 5.5 convert_reduce_fusion
  588.9 4.2 fusion.42
  593.2 0.2 convolution_dynamic-update-slice_fusion
  593.4 0.7 copy-done.10
  594.1 28.9 %all-reduce.6.cloned.1.call-done = f32[16,2048]{1,0:T(8,128)} async-done(((f32[16,2048]{1,0:T(8,128)}), f32[16,2048]{1,0:T(8,128)}) %all-reduce.6.cloned.1.call-update) | async-done | bytes 131088 | tf_op jit(solution)/shard_map/psum | solution.py:176
  623.1 73.2 %all-reduce.8.cloned.1.call-done = f32[16,2048]{1,0:T(8,128)} async-done(((f32[16,2048]{1,0:T(8,128)}), f32[16,2048]{1,0:T(8,128)}) %all-reduce.8.cloned.1.call-update) | async-done | bytes 131088 | tf_op jit(solution)/shard_map/psum | solution.py:176
  696.3 1.0 multiply_reduce_fusion.1
  697.3 8.4 %fusion.70 = (f32[16]{0:T(128)S(1)}, f32[16,3200]{1,0:T(8,128)S(1)}) fusion(bf16[3200,2048]{1,0:T(8,128)(2,1)} %param.27, f32[16,2048]{1,0:T(8,128)} %all-reduce.8.cloned.1.call-done, f32[2048]{0:T(1024)S(1)} %copy-done.14, f32[16]{0:T(128)S(1)} %add_rsqrt_fusion), kind=kOutput, calls=%fused_computation.115 | convolution fusion | flops 209864688 | bytes 13451392 | tf_op jit(solution)/shard_map/dot_general | solution.py:178
  705.8 0.7 copy-done.6
  706.4 0.2 exponential_reduce_fusion
  706.7 0.2 dynamic-update-slice
  706.9 0.2 dynamic-update-slice.1
  707.1 39.6 %all-reduce.2 = (f32[512]{0:T(512)S(1)}, f32[512]{0:T(512)S(1)}) all-reduce(f32[512]{0:T(512)S(1)} %dynamic-update-slice, f32[512]{0:T(512)S(1)} %dynamic-update-slice.1), channel_id=2, replica_groups=mesh['seq'=8,'exp'=4] {'seq','exp'}, use_global_device_ids=true, to_apply=%add | all-reduce | flops 1024 | bytes 8192
  747.0 1.3 while.23
  748.3 1.7 broadcast_subtract_fusion
  (110 shorter events, 2.6 us)
Async XLA Ops:
  7.2 400.9 %copy-start = (bf16[1,704,2048]{2,1,0:T(8,128)(2,1)S(1)}, bf16[1,704,2048]{2,1,0:T(8,128)(2,1)}, u32[]{:S(2)}) copy-start(bf16[1,704,2048]{2,1,0:T(8,128)(2,1)} %param.25) | copy-start | bytes 8650756
  7.2 79.7 %all-gather.5.cloned.1.call-start = ((), (), s32[]{:S(2)}) async-start(), calls=%async_computation.3 | async-start | bytes 4718592 | tf_op jit(solution)/shard_map/all_gather | solution.py:87
  10.7 209.9 %all-gather.7.cloned.1.call-start = ((), (), s32[]{:S(2)}) async-start(), calls=%async_computation.4 | async-start | bytes 9437184 | tf_op jit(solution)/shard_map/all_gather | solution.py:120
  12.3 12.9 %copy-start.15 = (s32[4,1]{0,1:T(1,128)}, s32[4,1]{0,1:T(1,128)S(1)}, u32[]{:S(2)}) copy-start(s32[4,1]{0,1:T(1,128)S(1)} %reduce-window.10) | copy-start | bytes 52
  20.3 4.8 copy-start.17
  93.1 1.9 copy-start.4
  98.4 28.4 %copy-start.13 = (s32[1,128,6]{1,0,2:T(1,128)S(1)}, s32[1,128,6]{1,0,2:T(1,128)}, u32[]{:S(2)}) copy-start(s32[1,128,6]{1,0,2:T(1,128)} %param.23) | copy-start | bytes 9220
  105.0 3.1 copy-start.8
  108.5 0.8 copy-start.9
  115.9 3.1 copy-start.8
  119.4 0.8 copy-start.9
  120.2 100.4 %copy-start.3 = (bf16[1,128,2048]{2,1,0:T(8,128)(2,1)S(1)}, bf16[1,128,2048]{2,1,0:T(8,128)(2,1)}, u32[]{:S(2)}) copy-start(bf16[1,128,2048]{2,1,0:T(8,128)(2,1)} %param.16) | copy-start | bytes 1572868
  122.5 23.0 %all-to-all-start = ((bf16[8,128,256]{2,1,0:T(8,128)(2,1)}), bf16[8,128,256]{2,1,0:T(8,128)(2,1)}, u32[]{:S(2)}, u32[]{:S(2)}) async-start(bf16[8,128,256]{2,1,0:T(8,128)(2,1)} %all_to_all.20), calls=%async_computation | async-start | bytes 1048576 | tf_op jit(solution)/shard_map/all_to_all | solution.py:119
  220.6 5.0 copy-start.12
  225.5 3.0 copy-start.1
  416.3 4.3 copy-start.16
  416.3 4.3 copy-start.11
  416.3 167.0 %all-to-all-start.2 = ((bf16[32,56,2048]{2,1,0:T(8,128)(2,1)}), bf16[32,56,2048]{2,1,0:T(8,128)(2,1)}, u32[]{:S(2)}, u32[]{:S(2)}) async-start(bf16[32,56,2048]{2,1,0:T(8,128)(2,1)} %bitcast.123), calls=%async_computation.2 | async-start | bytes 14680064 | tf_op jit(solution)/shard_map/all_to_all | solution.py:158
  420.3 202.8 %all-reduce.6.cloned.1.call-start = ((), (), s32[]{:S(2)}) async-start(), calls=%async_computation.5 | async-start | bytes 262144 | tf_op jit(solution)/shard_map/psum | solution.py:176
  583.4 5.5 copy-start.2
  583.4 5.5 copy-start.7
  588.9 108.4 %copy-start.14 = (f32[2048]{0:T(1024)S(1)}, f32[2048]{0:T(1024)}, u32[]{:S(2)}) copy-start(f32[2048]{0:T(1024)} %param.26) | copy-start | bytes 24580
  593.1 112.6 %copy-start.5 = (bf16[128,2048]{1,0:T(8,128)(2,1)}, bf16[128,2048]{1,0:T(8,128)(2,1)S(1)}, u32[]{:S(2)}) copy-start(bf16[128,2048]{1,0:T(8,128)(2,1)S(1)} %fusion.42) | copy-start | bytes 1572868
  593.4 0.7 copy-start.10
  594.1 102.2 %all-reduce.8.cloned.1.call-start = ((), (), s32[]{:S(2)}) async-start(), calls=%async_computation.6 | async-start | bytes 262144 | tf_op jit(solution)/shard_map/psum | solution.py:176
  705.7 0.7 copy-start.6
Sparse Core Ops, SparseCore 0:
  10.8 76.0 all-gather.4
  89.0 131.4 all-gather.6
  594.2 28.8 all-reduce.5
  626.6 69.5 all-reduce.7
